TPU v7x, 256 devices: a whole 4x4x8 slice. The times are simulated.
256 devices in a mesh: dp: 8 (over x, core), seq: 32 (over y, z).
Axes of the slice: x: 4, y: 4, z: 8, core: 2. Of those that a mesh axis runs over, the one named last changes fastest.
Arguments:
- activations: bfloat16 [8, 4096, 2048], P('dp', 'seq'), may hold values from -16 to 16
- w_query: bfloat16 [2048, 2048], P('seq')
- w_key: bfloat16 [2048, 256], P('seq')
- w_value: bfloat16 [2048, 256], P('seq'), may hold values from -0.125 to 0.125
- key_blocks: int32 [32, 32, 7], replicated, may hold values from 0 to 31, as said below
- random_count: int32 [32], replicated, may hold values from 1 to 3, 64 in all
- grad_out: bfloat16 [8, 4096, 2048], P('dp', 'seq'), may hold values from -6 to 6
Outputs:
- attn_out: bfloat16 [8, 4096, 2048], P('dp', 'seq')
- grad_x: bfloat16 [8, 4096, 2048], P('dp', 'seq')
- grad_wq: bfloat16 [2048, 2048], P('seq')
- grad_wk: bfloat16 [2048, 256], P('seq')
- grad_wv: bfloat16 [2048, 256], P('seq')
Inputs may be any that keep to these rules, and one draw needn't show every extreme that they name: `key_blocks`: row b of head h: columns 0 to 2 are b - 1, b and b + 1 modulo 32; column 3 is one block of the head, the same in all its rows; columns 4 to 6 are three blocks that differ from each other and from the row's first four entries. Head h uses the first random_count[h] of its three random key blocks; the counts sum to 64.
All inputs are finite; a program needn't handle non-finite values.
Results may differ from a plain program's by a relative error of at most 0.025.
The roundings to bfloat16 on the way count: a program that leaves them out, or rounds other values in their place, can miss the bound.
Values may be sent and summed in bfloat16 or wider, within the bound.
No kernel may reach another device: no remote copies, remote signals or barrier semaphores. Data moves between devices by JAX's collectives and lax.ppermute only.
A program may use at most 128 MiB of HBM per device.

v0:
```python
import math
import jax
import jax.numpy as jnp
from jax import lax
from jax.sharding import PartitionSpec as P

HD = 64
GROUP = 8
masked_score = -1e30
query_group = 4


def head_pass(queries, key_rows, value_rows, grad_head, blocks, extra_count):
    seq_len, head_width = queries.shape
    block_count, slot_count = blocks.shape
    block_len = seq_len // block_count
    score_scale = head_width ** (-0.5)
    key_tiles = key_rows.reshape(block_count, block_len, head_width)
    value_tiles = value_rows.reshape(block_count, block_len, head_width)
    usable = jnp.repeat(jnp.arange(slot_count) < 4 + extra_count, block_len)
    rounds = block_count // query_group
    query_steps = queries.reshape(rounds, query_group, block_len, head_width)
    grad_steps = grad_head.reshape(rounds, query_group, block_len, head_width)
    block_steps = blocks.reshape(rounds, query_group, slot_count)

    def one_step(running, inputs):
        q_part, g_part, chosen = inputs
        k_part = key_tiles[chosen].reshape(query_group, slot_count * block_len, head_width)
        v_part = value_tiles[chosen].reshape(query_group, slot_count * block_len, head_width)
        scores = (
            jnp.einsum("gqe,gke->gqk", q_part, k_part, preferred_element_type=jnp.float32)
            * score_scale
        )
        scores = jnp.where(usable, scores, masked_score)
        highest = jnp.max(scores, axis=-1, keepdims=True)
        exponent = jnp.exp(scores - highest)
        shares = exponent / jnp.sum(exponent, axis=-1, keepdims=True)
        shares_low = shares.astype(jnp.bfloat16)
        attended = jnp.einsum(
            "gqk,gke->gqe", shares_low, v_part, preferred_element_type=jnp.float32
        ).astype(jnp.bfloat16)
        grad_shares = jnp.einsum("gqe,gke->gqk", g_part, v_part, preferred_element_type=jnp.float32)
        weighted = jnp.sum(grad_shares * shares, axis=-1, keepdims=True)
        grad_scores = (shares * (grad_shares - weighted)).astype(jnp.bfloat16)
        grad_query = (
            jnp.einsum("gqk,gke->gqe", grad_scores, k_part, preferred_element_type=jnp.float32)
            * score_scale
        ).astype(jnp.bfloat16)
        grad_keys = (
            jnp.einsum("gqk,gqe->gke", grad_scores, q_part, preferred_element_type=jnp.float32)
            * score_scale
        )
        grad_values = jnp.einsum(
            "gqk,gqe->gke", shares_low, g_part, preferred_element_type=jnp.float32
        )
        pieces = jnp.concatenate([grad_keys, grad_values], axis=-1).reshape(
            query_group * slot_count, block_len, 2 * head_width
        )
        running = running.at[chosen.reshape(-1)].add(pieces)
        return (running, (attended, grad_query))

    initial = jnp.zeros((block_count, block_len, 2 * head_width), jnp.float32)
    summed, (attended, grad_query) = lax.scan(
        one_step, initial, (query_steps, grad_steps, block_steps)
    )
    return (
        attended.reshape(seq_len, head_width),
        grad_query.reshape(seq_len, head_width),
        summed.reshape(seq_len, 2 * head_width),
    )


def per_device(activations, w_query, w_key, w_value, key_blocks, random_count, grad_out):
    seq_devices = lax.axis_size("seq")
    dp_devices = lax.axis_size("dp")
    position = lax.axis_index("seq")
    dp_index = lax.axis_index("dp")
    tokens = activations[0]
    grad_rows = grad_out[0]
    tok_count = tokens.shape[0]
    heads = w_query.shape[1] // HD
    kv_heads = w_key.shape[1] // HD
    query_cols = heads * HD
    kv_cols = kv_heads * HD
    all_cols = query_cols + 2 * kv_cols
    w_local = jnp.concatenate([w_query, w_key, w_value], axis=1)
    w_full = lax.all_gather(w_local, "seq", axis=0, tiled=True)
    projected = jnp.dot(tokens, w_full, preferred_element_type=jnp.float32).astype(jnp.bfloat16)
    queries = projected[:, :query_cols]
    key_proj = projected[:, query_cols : query_cols + kv_cols]
    value_proj = projected[:, query_cols + kv_cols :]
    query_pieces = queries.reshape(tok_count, heads, HD).transpose(1, 0, 2)
    grad_pieces = grad_rows.reshape(tok_count, heads, HD).transpose(1, 0, 2)
    paired = jnp.concatenate(
        [key_proj.reshape(tok_count, kv_heads, HD), value_proj.reshape(tok_count, kv_heads, HD)],
        axis=2,
    )
    kv_pieces = jnp.repeat(paired.transpose(1, 0, 2), GROUP, axis=0)
    sent = jnp.concatenate([query_pieces, grad_pieces, kv_pieces], axis=2)
    landed = lax.all_to_all(sent, "seq", split_axis=0, concat_axis=1, tiled=True)[0]
    head_q = landed[:, :HD]
    head_grad = landed[:, HD : 2 * HD]
    head_k = landed[:, 2 * HD : 3 * HD]
    head_v = landed[:, 3 * HD :]
    blocks_mine = lax.dynamic_index_in_dim(key_blocks, position, 0, keepdims=False)
    count_mine = lax.dynamic_index_in_dim(random_count, position, 0, keepdims=False)
    attended, grad_query, grad_kv = head_pass(
        head_q, head_k, head_v, head_grad, blocks_mine, count_mine
    )
    back_sent = jnp.concatenate(
        [
            attended.reshape(seq_devices, tok_count, HD),
            grad_query.reshape(seq_devices, tok_count, HD),
            grad_kv.astype(jnp.bfloat16).reshape(seq_devices, tok_count, 2 * HD),
        ],
        axis=2,
    )
    back = lax.all_to_all(back_sent, "seq", split_axis=0, concat_axis=0, tiled=True)
    back_out = back[:, :, :HD]
    back_query = back[:, :, HD : 2 * HD]
    back_kv = back[:, :, 2 * HD :]
    out_rows = back_out.transpose(1, 0, 2).reshape(tok_count, heads * HD)
    grad_q_rows = back_query.transpose(1, 0, 2).reshape(tok_count, heads * HD)
    kv_sum = jnp.sum(
        back_kv.reshape(kv_heads, GROUP, tok_count, 2 * HD), axis=1, dtype=jnp.float32
    ).astype(jnp.bfloat16)
    grad_k_rows = kv_sum[:, :, :HD].transpose(1, 0, 2).reshape(tok_count, kv_heads * HD)
    grad_v_rows = kv_sum[:, :, HD:].transpose(1, 0, 2).reshape(tok_count, kv_heads * HD)
    combined = jnp.concatenate([grad_q_rows, grad_k_rows, grad_v_rows], axis=1)
    contract = (((1,), (1,)), ((), ()))
    grad_x_rows = lax.dot_general(
        combined, w_full, contract, preferred_element_type=jnp.float32
    ).astype(jnp.bfloat16)
    factor = 1.0 / math.sqrt(tok_count * seq_devices * dp_devices)
    over_tokens = (((0,), (0,)), ((), ()))
    term = (
        lax.dot_general(tokens, combined, over_tokens, preferred_element_type=jnp.float32) * factor
    ).astype(jnp.bfloat16)
    half = all_cols // 2
    core = dp_index % 2
    pairs = [(i, i ^ 1) for i in range(dp_devices)]
    keep = lax.dynamic_slice_in_dim(term, core * half, half, axis=1)
    give = lax.dynamic_slice_in_dim(term, (1 - core) * half, half, axis=1)
    got = lax.ppermute(give, "dp", pairs)
    chip_sum = (keep.astype(jnp.float32) + got.astype(jnp.float32)).astype(jnp.bfloat16)
    part = lax.psum_scatter(chip_sum, "seq", scatter_dimension=0, tiled=True)
    step = 2
    while step < dp_devices:
        mates = [(i, i ^ step) for i in range(dp_devices)]
        other = lax.ppermute(part, "dp", mates)
        part = (part.astype(jnp.float32) + other.astype(jnp.float32)).astype(jnp.bfloat16)
        step *= 2
    other_half = lax.ppermute(part, "dp", pairs)
    first = jnp.where(core == 0, part, other_half)
    second = jnp.where(core == 0, other_half, part)
    grad_all = jnp.concatenate([first, second], axis=1)
    grad_wq = grad_all[:, :query_cols]
    grad_wk = grad_all[:, query_cols : query_cols + kv_cols]
    grad_wv = grad_all[:, query_cols + kv_cols :]
    return (out_rows[None], grad_x_rows[None], grad_wq, grad_wk, grad_wv)


def solution(mesh):
    placed = (
        P("dp", "seq", None),
        P("seq", None),
        P("seq", None),
        P("seq", None),
        P(),
        P(),
        P("dp", "seq", None),
    )
    return jax.shard_map(
        per_device,
        mesh=mesh,
        in_specs=placed,
        out_specs=(
            P("dp", "seq", None),
            P("dp", "seq", None),
            P("seq", None),
            P("seq", None),
            P("seq", None),
        ),
        check_vma=False,
    )
```

profile of v0, /device:TPU:7, one launch (start us, length us, event | category | flops | bytes accessed | tf_op | source)
XLA Modules:
  0.0 728.5 jit_solution(3099953773682184216)
XLA Ops:
  10.4 112.5 %all-gather.2.cloned.1.call-done = bf16[2048,2560]{1,0:T(8,128)(2,1)} async-done(((bf16[64,2560]{1,0:T(8,128)(2,1)}), bf16[2048,2560]{1,0:T(8,128)(2,1)}) %all-gather.2.cloned.1.call-update) | async-done | bytes 10485776 | tf_op jit(solution)/shard_map/all_gather | solution.py:87
  122.8 6.9 fusion.43
  131.6 5.4 all-to-all-start
  139.2 46.5 %all-to-all-done = bf16[32,128,256]{1,2,0:T(8,128)(2,1)S(1)} async-done(((bf16[32,128,256]{1,2,0:T(8,128)(2,1)}), bf16[32,128,256]{1,2,0:T(8,128)(2,1)S(1)}, u32[]{:S(2)}, u32[]{:S(2)}) %all-to-all-start) | async-done | bytes 2097184 | tf_op jit(solution)/shard_map/all_to_all | solution.py:100
  199.0 167.2 %while.15 = (s32[]{:T(128)}, f32[32,128,128]{2,1,0:T(8,128)}, bf16[8,4,128,64]{2,3,1,0:T(8,128)(2,1)}, bf16[8,4,128,64]{2,3,1,0:T(8,128)(2,1)}, s32[8,4,7]{2,1,0...) while((s32[]{:T(128)}, f32[32,128,128]{2,1,0:T(8,128)}, ...), condition=%wide.region_5.6_spmd.clone, body=%wide.region_0.5_spmd.clone.sunk | while | flops 360449568 | bytes 45045204 | solution.py:63
  213.1 6.9 scatter_fusion
  234.0 6.9 scatter_fusion
  254.9 6.8 scatter_fusion
  275.8 6.8 scatter_fusion
  296.7 6.9 scatter_fusion
  317.6 6.8 scatter_fusion
  338.5 6.8 scatter_fusion
  359.4 6.8 scatter_fusion
  369.7 7.2 all-to-all-start.1
  377.1 49.0 %all-to-all-done.1 = bf16[32,128,256]{1,2,0:T(8,128)(2,1)S(1)} async-done(((bf16[32,128,256]{1,2,0:T(8,128)(2,1)}), bf16[32,128,256]{1,2,0:T(8,128)(2,1)S(1)}, u32[]{:S(2)}, u32[]{:S(2)}) %all-to-all-start.1) | async-done | bytes 2097184 | tf_op jit(solution)/shard_map/all_to_all | solution.py:118
  427.2 5.1 multiply_convert_fusion.1
  439.7 8.6 %collective-permute-done = bf16[2048,1280]{0,1:T(8,128)(2,1)} collective-permute-done((bf16[2048,1280]{0,1:T(8,128)(2,1)}, bf16[2048,1280]{0,1:T(8,128)(2,1)}, u32[]{:S(2)}, u32[]{:S(2)}) %collective-permute-start) | collective-permute-done | bytes 5242912 | tf_op jit(solution)/shard_map/ppermute | solution.py:144
  448.3 9.4 %fusion.42 = bf16[2048,1280]{0,1:T(8,128)(2,1)} fusion(bf16[2048,1280]{0,1:T(8,128)(2,1)} %collective-permute-done, bf16[2560,2048]{1,0:T(8,128)(2,1)} %copy-done.1, s32[]{:T(128)S(6)} %select_n.59), kind=kLoop, calls=%fused_computation.54 | loop fusion | flops 10485760 | bytes 15728644 | tf_op jit(solution)/shard_map/convert_element_type | solution.py:145
  457.7 7.9 %copy.86 = bf16[2048,1280]{1,0:T(8,128)(2,1)} copy(bf16[2048,1280]{0,1:T(8,128)(2,1)} %fusion.42) | data formatting | bytes 10485760
  465.7 218.4 %reduce-scatter.4.cloned.1.call-done = bf16[64,1280]{1,0:T(8,128)(2,1)} async-done(((bf16[2048,1280]{1,0:T(8,128)(2,1)}), bf16[64,1280]{1,0:T(8,128)(2,1)}) %reduce-scatter.4.cloned.1.call-update) | async-done | bytes 163856
  685.5 5.7 collective-permute-done.1
  692.1 8.1 %collective-permute-done.2 = bf16[64,1280]{0,1:T(8,128)(2,1)S(1)} collective-permute-done((bf16[64,1280]{0,1:T(8,128)(2,1)S(1)}, bf16[64,1280]{0,1:T(8,128)(2,1)S(1)}, u32[]{:S(2)}, u32[]{:S(2)}) %collective-permute-start.2) | collective-permute-done | bytes 163872 | tf_op jit(solution)/shard_map/ppermute | solution.py:150
  700.4 9.5 %collective-permute-start.3 = (bf16[64,1280]{0,1:T(8,128)(2,1)S(1)}, bf16[64,1280]{0,1:T(8,128)(2,1)S(1)}, u32[]{:S(2)}, u32[]{:S(2)}) collective-permute-start(bf16[64,1280]{0,1:T(8,128)(2,1)S(1)} %add_convert_fusion), channel_id=1, source_target_pairs={{0,32},{32,0},{64,96},{96,64},{128,160},{160,128},{192,224},{224,1... | collective-permute-start | bytes 491528 | tf_op jit(solution)/shard_map/ppermute | solution.py:153
  709.9 8.3 %fusion.44 = bf16[1,128,2048]{2,1,0:T(8,128)(2,1)} fusion(bf16[2048,2560]{1,0:T(8,128)(2,1)} %all-gather.2.cloned.1.call-done, bf16[128,256]{0,1:T(8,128)(2,1)S(1)} %bitcast.151, bf16[128,256]{0,1:T(8,128)(2,1)S(1)} %bitcast.149, bf16[128,2048]{0,1:T(8,128)(2,1)S(1)} %bitcast.141), kind=kOutput, calls=%fused_computation.59 | convolution fusion | flops 1344405504 | bytes 11665408 | tf_op jit(solution)/shard_map/dot_general | solution.py:131
  (270 shorter events, 149.7 us)
Async XLA Ops:
  7.2 115.7 %copy-start = (bf16[1,128,2048]{2,1,0:T(8,128)(2,1)S(1)}, bf16[1,128,2048]{2,1,0:T(8,128)(2,1)}, u32[]{:S(2)}) copy-start(bf16[1,128,2048]{2,1,0:T(8,128)(2,1)} %param.9) | copy-start | bytes 1572868
  7.2 115.7 %all-gather.2.cloned.1.call-start = ((), (), s32[]{:S(2)}) async-start(), calls=%async_computation.3 | async-start | bytes 10813440 | tf_op jit(solution)/shard_map/all_gather | solution.py:87
  131.6 54.1 %all-to-all-start = ((bf16[32,128,256]{1,2,0:T(8,128)(2,1)}), bf16[32,128,256]{1,2,0:T(8,128)(2,1)S(1)}, u32[]{:S(2)}, u32[]{:S(2)}) async-start(bf16[32,128,256]{1,2,0:T(8,128)(2,1)} %pad_maximum_fusion.1), calls=%async_computation | async-start | bytes 4194304 | tf_op jit(solution)/shard_map/all_to_all | solution.py:100
  213.1 6.9 copy-start.3
  213.1 6.9 copy-start.5
  234.0 6.9 copy-start.3
  234.0 6.9 copy-start.5
  254.9 6.8 copy-start.5
  275.8 6.8 copy-start.3
  275.8 6.8 copy-start.5
  296.7 6.9 copy-start.3
  296.7 6.9 copy-start.5
  317.6 6.8 copy-start.5
  338.5 6.8 copy-start.3
  338.5 6.8 copy-start.5
  359.4 6.8 copy-start.3
  359.4 6.8 copy-start.5
  369.7 56.4 %all-to-all-start.1 = ((bf16[32,128,256]{1,2,0:T(8,128)(2,1)}), bf16[32,128,256]{1,2,0:T(8,128)(2,1)S(1)}, u32[]{:S(2)}, u32[]{:S(2)}) async-start(bf16[32,128,256]{1,2,0:T(8,128)(2,1)} %pad_maximum_fusion.2), calls=%async_computation.1 | async-start | bytes 4194304 | tf_op jit(solution)/shard_map/all_to_all | solution.py:118
  376.9 307.2 %reduce-scatter.4.cloned.1.call-start = ((), (), s32[]{:S(2)}) async-start(), calls=%async_computation.4 | async-start | bytes 5406720
  437.8 10.6 %collective-permute-start = (bf16[2048,1280]{0,1:T(8,128)(2,1)}, bf16[2048,1280]{0,1:T(8,128)(2,1)}, u32[]{:S(2)}, u32[]{:S(2)}) collective-permute-start(bf16[2048,1280]{0,1:T(8,128)(2,1)} %dynamic-slice_bitcast_fusion), channel_id=1, source_target_pairs={{0,32},{32,0},{64,96},{96,64},{128,160},{160,128},{192,224},{224,1... | collective-permute-start | bytes 15728648 | tf_op jit(solution)/shard_map/ppermute | solution.py:144
  685.2 6.0 collective-permute-start.1
  691.3 9.0 %collective-permute-start.2 = (bf16[64,1280]{0,1:T(8,128)(2,1)S(1)}, bf16[64,1280]{0,1:T(8,128)(2,1)S(1)}, u32[]{:S(2)}, u32[]{:S(2)}) collective-permute-start(bf16[64,1280]{0,1:T(8,128)(2,1)S(1)} %add_convert_fusion.1), channel_id=1, source_target_pairs={{0,128},{32,160},{64,192},{96,224},{128,0},{160,32},{192,64},{224,... | collective-permute-start | bytes 491528 | tf_op jit(solution)/shard_map/ppermute | solution.py:150
  700.4 17.8 %copy-start.7 = (bf16[32,128,64]{1,2,0:T(8,128)(2,1)S(1)}, bf16[32,128,64]{1,2,0:T(8,128)(2,1)}, u32[]{:S(2)}) copy-start(bf16[32,128,64]{1,2,0:T(8,128)(2,1)} %get-tuple-element.162) | copy-start | bytes 1572868
  700.4 18.8 %collective-permute-start.3 = (bf16[64,1280]{0,1:T(8,128)(2,1)S(1)}, bf16[64,1280]{0,1:T(8,128)(2,1)S(1)}, u32[]{:S(2)}, u32[]{:S(2)}) collective-permute-start(bf16[64,1280]{0,1:T(8,128)(2,1)S(1)} %add_convert_fusion), channel_id=1, source_target_pairs={{0,32},{32,0},{64,96},{96,64},{128,160},{160,128},{192,224},{224,1... | collective-permute-start | bytes 491528 | tf_op jit(solution)/shard_map/ppermute | solution.py:153
  (30 other events, 75.9 us)
Sparse Core Ops, SparseCore 0:
  11.2 111.6 all-gather.1
  465.8 218.2 reduce-scatter.3
where the time goes:
time: 731 us; the launch traced here: 729 us
  waiting for transfers between devices  449 us (61%)
  matrix products  93.4 us (13%)
  other arithmetic  73.4 us (10%)
  local copies, waits for them, and re-layouts  72 us (10%)
  starting transfers between devices  25.4 us (3%)
  between operations  14.9 us (2%)
    unnamed x3, waiting for transfers between devices  218 us
    all_gather x1, waiting for transfers between devices, per_device(): w_full = lax.all_gather(w_local, 'seq', axis=0, tiled=True)  112 us
    scatter-add x8, other arithmetic, one_step(): running = running.at[chosen.reshape(-1)].add(pieces)  54.7 us
    all_to_all x1, waiting for transfers between devices, per_device(): lax.all_to_all(back_sent, 'seq', split_axis=0, concat_axis=0, tiled=True)  49 us
    all_to_all x1, waiting for transfers between devices, per_device(): lax.all_to_all(sent, 'seq', split_axis=0, concat_axis=1, tiled=True)[0]  46.5 us
    unnamed x21, local copies, waits for them, and re-layouts  20.6 us
    dot_general x8, matrix products, one_step(): jnp.einsum('gqk,gke->gqe', shares_low, v_part, preferred_element_type=jnp...  19.1 us
  transfers between devices with their start and end apart: 8, of which 7 were waited for; matrix products, arithmetic and copies ran while one was open for 2% of the time, Pallas kernels for 0%

commit v1 on v0

--- a/solution.py
+++ b/solution.py
@@ -84,7 +84,9 @@
     kv_cols = kv_heads * HD
     all_cols = query_cols + 2 * kv_cols
     w_local = jnp.concatenate([w_query, w_key, w_value], axis=1)
-    w_full = lax.all_gather(w_local, "seq", axis=0, tiled=True)
+    w_full = jnp.concatenate(
+        lax.all_to_all(jnp.stack([w_local] * lax.axis_size("seq")), "seq", 0, 0), axis=0
+    )
     projected = jnp.dot(tokens, w_full, preferred_element_type=jnp.float32).astype(jnp.bfloat16)
     queries = projected[:, :query_cols]
     key_proj = projected[:, query_cols : query_cols + kv_cols]

time: 731 us -> 879 us (1.20)
  waiting for transfers between devices: 449 us -> 573 us
  starting transfers between devices: 25.4 us -> 45.8 us
    all_to_all x0 -> x1, waiting for transfers between devices: none -> 238 us  [per_device(): lax.all_to_all(jnp.stack([w_local] * lax.axis_size('seq')), 'seq', 0, 0)]
    all_gather x1 -> x0, waiting for transfers between devices: 112 us -> none  [per_device(): w_full = lax.all_gather(w_local, 'seq', axis=0, tiled=True)]
    all_to_all x0 -> x1, starting transfers between devices: none -> 11.4 us  [per_device(): lax.all_to_all(jnp.stack([w_local] * lax.axis_size('seq')), 'seq', 0, 0)]
    unnamed x21 -> x23, local copies, waits for them, and re-layouts: 20.6 us -> 19.6 us
    unnamed x3 -> x2, waiting for transfers between devices: 218 us -> 218 us
  transfers between devices with their start and end apart: 8 -> 8, of which waited for: 7 -> 7; matrix products, arithmetic and copies ran while one was open for 2% -> 1% of each run, Pallas kernels for 0% -> 0%
where the time goes in v1:
time: 879 us; the launch traced here: 876 us
  waiting for transfers between devices  573 us (65%)
  matrix products  93.3 us (11%)
  local copies, waits for them, and re-layouts  75.9 us (9%)
  other arithmetic  72.7 us (8%)
  starting transfers between devices  45.8 us (5%)
  between operations  14.9 us (2%)
    all_to_all x1, waiting for transfers between devices, per_device(): lax.all_to_all(jnp.stack([w_local] * lax.axis_size('seq')), 'seq', 0, 0)  238 us
    unnamed x2, waiting for transfers between devices  218 us
    scatter-add x8, other arithmetic, one_step(): running = running.at[chosen.reshape(-1)].add(pieces)  54.7 us
    all_to_all x1, waiting for transfers between devices, per_device(): lax.all_to_all(back_sent, 'seq', split_axis=0, concat_axis=0, tiled=True)  48.6 us
    all_to_all x1, waiting for transfers between devices, per_device(): lax.all_to_all(sent, 'seq', split_axis=0, concat_axis=1, tiled=True)[0]  46.5 us
    unnamed x23, local copies, waits for them, and re-layouts  19.6 us
    dot_general x8, matrix products, one_step(): jnp.einsum('gqk,gke->gqe', shares_low, v_part, preferred_element_type=jnp...  19.1 us
  transfers between devices with their start and end apart: 8, of which 7 were waited for; matrix products, arithmetic and copies ran while one was open for 1% of the time, Pallas kernels for 0%

profile of v1, /device:TPU:7, one launch (start us, length us, event | category | flops | bytes accessed | tf_op | source)
XLA Modules:
  0.0 876.1 jit_solution(1736680714293335547)
XLA Ops:
  13.3 11.4 %all-to-all-start = ((bf16[32,64,2560]{2,1,0:T(8,128)(2,1)}), bf16[32,64,2560]{2,1,0:T(8,128)(2,1)}, u32[]{:S(2)}, u32[]{:S(2)}) async-start(bf16[32,64,2560]{2,1,0:T(8,128)(2,1)} %stack.2), calls=%async_computation | async-start | bytes 20971520 | tf_op jit(solution)/shard_map/all_to_all | solution.py:88
  25.0 237.8 %all-to-all-done = bf16[32,64,2560]{2,1,0:T(8,128)(2,1)} async-done(((bf16[32,64,2560]{2,1,0:T(8,128)(2,1)}), bf16[32,64,2560]{2,1,0:T(8,128)(2,1)}, u32[]{:S(2)}, u32[]{:S(2)}) %all-to-all-start) | async-done | bytes 10485792 | tf_op jit(solution)/shard_map/all_to_all | solution.py:88
  262.8 6.9 fusion.43
  271.6 13.3 %all-to-all-start.1 = ((bf16[32,128,256]{1,2,0:T(8,128)(2,1)}), bf16[32,128,256]{1,2,0:T(8,128)(2,1)S(1)}, u32[]{:S(2)}, u32[]{:S(2)}) async-start(bf16[32,128,256]{1,2,0:T(8,128)(2,1)} %pad_maximum_fusion.1), calls=%async_computation.1 | async-start | bytes 4194304 | tf_op jit(solution)/shard_map/all_to_all | solution.py:102
  287.0 46.5 %all-to-all-done.1 = bf16[32,128,256]{1,2,0:T(8,128)(2,1)S(1)} async-done(((bf16[32,128,256]{1,2,0:T(8,128)(2,1)}), bf16[32,128,256]{1,2,0:T(8,128)(2,1)S(1)}, u32[]{:S(2)}, u32[]{:S(2)}) %all-to-all-start.1) | async-done | bytes 2097184 | tf_op jit(solution)/shard_map/all_to_all | solution.py:102
  346.8 167.1 %while.15 = (s32[]{:T(128)}, f32[32,128,128]{2,1,0:T(8,128)}, bf16[8,4,128,64]{2,3,1,0:T(8,128)(2,1)}, bf16[8,4,128,64]{2,3,1,0:T(8,128)(2,1)}, s32[8,4,7]{2,1,0...) while((s32[]{:T(128)}, f32[32,128,128]{2,1,0:T(8,128)}, ...), condition=%wide.region_5.6_spmd.clone, body=%wide.region_0.5_spmd.clone.sunk | while | flops 360449568 | bytes 45045204 | solution.py:63
  360.9 6.9 scatter_fusion
  381.8 6.9 scatter_fusion
  402.7 6.8 scatter_fusion
  423.6 6.8 scatter_fusion
  444.4 6.9 scatter_fusion
  465.4 6.8 scatter_fusion
  486.2 6.8 scatter_fusion
  507.1 6.8 scatter_fusion
  517.4 7.2 all-to-all-start.2
  524.6 48.6 %all-to-all-done.2 = bf16[32,128,256]{1,2,0:T(8,128)(2,1)S(1)} async-done(((bf16[32,128,256]{1,2,0:T(8,128)(2,1)}), bf16[32,128,256]{1,2,0:T(8,128)(2,1)S(1)}, u32[]{:S(2)}, u32[]{:S(2)}) %all-to-all-start.2) | async-done | bytes 2097184 | tf_op jit(solution)/shard_map/all_to_all | solution.py:120
  587.3 8.6 collective-permute-done
  595.9 9.4 %fusion.42 = bf16[2048,1280]{0,1:T(8,128)(2,1)} fusion(bf16[2048,1280]{0,1:T(8,128)(2,1)} %collective-permute-done, bf16[2560,2048]{1,0:T(8,128)(2,1)} %copy-done.1, s32[]{:T(128)S(6)} %select_n.59), kind=kLoop, calls=%fused_computation.54 | loop fusion | flops 10485760 | bytes 15728644 | tf_op jit(solution)/shard_map/convert_element_type | solution.py:147
  605.4 7.9 copy.86
  613.3 218.4 %reduce-scatter.4.cloned.1.call-done = bf16[64,1280]{1,0:T(8,128)(2,1)} async-done(((bf16[2048,1280]{1,0:T(8,128)(2,1)}), bf16[64,1280]{1,0:T(8,128)(2,1)}) %reduce-scatter.4.cloned.1.call-update) | async-done | bytes 163856
  833.4 5.3 collective-permute-done.1
  840.1 7.7 collective-permute-done.2
  848.0 9.5 %collective-permute-start.3 = (bf16[64,1280]{0,1:T(8,128)(2,1)S(1)}, bf16[64,1280]{0,1:T(8,128)(2,1)S(1)}, u32[]{:S(2)}, u32[]{:S(2)}) collective-permute-start(bf16[64,1280]{0,1:T(8,128)(2,1)S(1)} %add_convert_fusion), channel_id=1, source_target_pairs={{0,32},{32,0},{64,96},{96,64},{128,160},{160,128},{192,224},{224,1... | collective-permute-start | bytes 491528 | tf_op jit(solution)/shard_map/ppermute | solution.py:155
  857.5 8.3 fusion.44
  (272 shorter events, 159.1 us)
Async XLA Ops:
  7.2 255.6 %copy-start = (bf16[1,128,2048]{2,1,0:T(8,128)(2,1)S(1)}, bf16[1,128,2048]{2,1,0:T(8,128)(2,1)}, u32[]{:S(2)}) copy-start(bf16[1,128,2048]{2,1,0:T(8,128)(2,1)} %param.9) | copy-start | bytes 1572868
  13.3 11.5 %copy-start.8 = (bf16[1,128,2048]{2,1,0:T(8,128)(2,1)S(1)}, bf16[1,128,2048]{2,1,0:T(8,128)(2,1)}, u32[]{:S(2)}) copy-start(bf16[1,128,2048]{2,1,0:T(8,128)(2,1)} %param.15) | copy-start | bytes 1572868
  13.3 249.5 %all-to-all-start = ((bf16[32,64,2560]{2,1,0:T(8,128)(2,1)}), bf16[32,64,2560]{2,1,0:T(8,128)(2,1)}, u32[]{:S(2)}, u32[]{:S(2)}) async-start(bf16[32,64,2560]{2,1,0:T(8,128)(2,1)} %stack.2), calls=%async_computation | async-start | bytes 20971520 | tf_op jit(solution)/shard_map/all_to_all | solution.py:88
  271.5 13.3 %copy-start.11 = (s32[32]{0:T(128)S(1)}, s32[32]{0:T(128)}, u32[]{:S(2)}) copy-start(s32[32]{0:T(128)} %param.14) | copy-start | bytes 388
  271.6 61.9 %all-to-all-start.1 = ((bf16[32,128,256]{1,2,0:T(8,128)(2,1)}), bf16[32,128,256]{1,2,0:T(8,128)(2,1)S(1)}, u32[]{:S(2)}, u32[]{:S(2)}) async-start(bf16[32,128,256]{1,2,0:T(8,128)(2,1)} %pad_maximum_fusion.1), calls=%async_computation.1 | async-start | bytes 4194304 | tf_op jit(solution)/shard_map/all_to_all | solution.py:102
  360.9 6.9 copy-start.3
  360.9 6.9 copy-start.5
  381.8 6.9 copy-start.3
  381.8 6.9 copy-start.5
  423.5 6.8 copy-start.3
  423.6 6.8 copy-start.5
  444.4 6.9 copy-start.3
  444.4 6.9 copy-start.5
  486.2 6.8 copy-start.3
  486.2 6.8 copy-start.5
  507.1 6.8 copy-start.3
  507.1 6.8 copy-start.5
  517.4 55.8 %all-to-all-start.2 = ((bf16[32,128,256]{1,2,0:T(8,128)(2,1)}), bf16[32,128,256]{1,2,0:T(8,128)(2,1)S(1)}, u32[]{:S(2)}, u32[]{:S(2)}) async-start(bf16[32,128,256]{1,2,0:T(8,128)(2,1)} %pad_maximum_fusion.2), calls=%async_computation.2 | async-start | bytes 4194304 | tf_op jit(solution)/shard_map/all_to_all | solution.py:120
  524.6 307.1 %reduce-scatter.4.cloned.1.call-start = ((), (), s32[]{:S(2)}) async-start(), calls=%async_computation.4 | async-start | bytes 5406720
  584.8 11.1 %collective-permute-start = (bf16[2048,1280]{0,1:T(8,128)(2,1)}, bf16[2048,1280]{0,1:T(8,128)(2,1)}, u32[]{:S(2)}, u32[]{:S(2)}) collective-permute-start(bf16[2048,1280]{0,1:T(8,128)(2,1)} %dynamic-slice_bitcast_fusion), channel_id=1, source_target_pairs={{0,32},{32,0},{64,96},{96,64},{128,160},{160,128},{192,224},{224,1... | collective-permute-start | bytes 15728648 | tf_op jit(solution)/shard_map/ppermute | solution.py:146
  832.8 6.0 collective-permute-start.1
  838.9 9.0 %collective-permute-start.2 = (bf16[64,1280]{0,1:T(8,128)(2,1)S(1)}, bf16[64,1280]{0,1:T(8,128)(2,1)S(1)}, u32[]{:S(2)}, u32[]{:S(2)}) collective-permute-start(bf16[64,1280]{0,1:T(8,128)(2,1)S(1)} %add_convert_fusion.1), channel_id=1, source_target_pairs={{0,128},{32,160},{64,192},{96,224},{128,0},{160,32},{192,64},{224,... | collective-permute-start | bytes 491528 | tf_op jit(solution)/shard_map/ppermute | solution.py:152
  847.9 17.8 %copy-start.7 = (bf16[32,128,64]{1,2,0:T(8,128)(2,1)S(1)}, bf16[32,128,64]{1,2,0:T(8,128)(2,1)}, u32[]{:S(2)}) copy-start(bf16[32,128,64]{1,2,0:T(8,128)(2,1)} %get-tuple-element.162) | copy-start | bytes 1572868
  848.0 18.8 %collective-permute-start.3 = (bf16[64,1280]{0,1:T(8,128)(2,1)S(1)}, bf16[64,1280]{0,1:T(8,128)(2,1)S(1)}, u32[]{:S(2)}, u32[]{:S(2)}) collective-permute-start(bf16[64,1280]{0,1:T(8,128)(2,1)S(1)} %add_convert_fusion), channel_id=1, source_target_pairs={{0,32},{32,0},{64,96},{96,64},{128,160},{160,128},{192,224},{224,1... | collective-permute-start | bytes 491528 | tf_op jit(solution)/shard_map/ppermute | solution.py:155
  (31 other events, 84.1 us)
Sparse Core Ops, SparseCore 0:
  613.4 218.1 reduce-scatter.3
